TPU v7x, 256 devices: a whole 4x4x8 slice. The times are simulated.
256 devices in a mesh: space: 64 (over z, x, core), head: 4 (over y).
Axes of the slice: x: 4, y: 4, z: 8, core: 2. Of those that a mesh axis runs over, the one named last changes fastest.
Arguments:
- features: bfloat16 [512, 16, 16, 128], P('space', None, None, 'head'), may hold values from -6 to 6
- mask: int32 [512, 16, 16], P('space'), may hold values from 0 to 1, as said below
- conv1_weight: bfloat16 [27, 128, 128], replicated, may hold values from -0.21875 to 0.21875
- conv2_weight: bfloat16 [27, 128, 128], replicated, may hold values from -0.21875 to 0.21875
- down_weight: bfloat16 [8, 128, 512], replicated, may hold values from -0.1875 to 0.1875
- norm_gain: float32 [512], replicated, may hold values from 0.1 to 1.9
- qkv_weight: bfloat16 [512, 3, 512], P(None, None, 'head'), may hold values from -2 to 2
- out_weight: bfloat16 [512, 512], P('head'), may hold values from -0.25 to 0.25
Outputs:
- refined: bfloat16 [512, 16, 16, 128], P('space', None, None, 'head')
- level_out: bfloat16 [16384, 512], P('space', 'head')
Inputs may be any that keep to these rules, and one draw needn't show every extreme that they name: `mask`: A voxel is occupied only inside an active brick of 8^3 aligned voxels; the first brick and its first voxel are always occupied.
All inputs are finite; a program needn't handle non-finite values.
Results may differ from a plain program's by a relative error of at most 0.012.
Values may be sent and summed in bfloat16 or wider, within the bound.
No kernel may reach another device: no remote copies, remote signals or barrier semaphores. Data moves between devices by JAX's collectives and lax.ppermute only.
A program may use at most 64 MiB of HBM per device.

v0:
```python
import jax
import jax.numpy as jnp
from jax import lax
from jax.sharding import PartitionSpec as P

HEADS = 8
KEY_BLOCK = 1024


def with_halo(cells, axis, width):
    count = lax.axis_size(axis)
    ends = count - 1
    head = lax.slice_in_dim(cells, 0, width, axis=0)
    tail = lax.slice_in_dim(cells, cells.shape[0] - width, cells.shape[0], axis=0)
    return jnp.concatenate(
        [
            lax.ppermute(tail, axis, [(i, i + 1) for i in range(ends)]),
            cells,
            lax.ppermute(head, axis, [(i + 1, i) for i in range(ends)]),
        ],
        axis=0,
    )


def convolve(rimmed, weight):
    chans = weight.shape[1]
    kernel = weight.reshape(3, 3, 3, chans, weight.shape[2])
    out = lax.conv_general_dilated(
        rimmed[None],
        kernel,
        window_strides=(1, 1, 1),
        padding=((0, 0), (1, 1), (1, 1)),
        dimension_numbers=("NDHWC", "DHWIO", "NDHWC"),
        preferred_element_type=jnp.float32,
    )
    return out[0]


def to_cells(field):
    nx, ny, nz, count = field.shape
    blocks = field.reshape(nx // 2, 2, ny // 2, 2, nz // 2, 2, count).transpose(0, 2, 4, 1, 3, 5, 6)
    return blocks.reshape(nx // 2 * (ny // 2) * (nz // 2), 8 * count)


def body(
    features, mask, conv1_weight, conv2_weight, down_weight, norm_gain, qkv_weight, out_weight
):
    member = lax.axis_index("head")
    nx, ny, nz, local = features.shape
    width = down_weight.shape[2]
    chans = conv1_weight.shape[1]
    tokens = nx // 2 * (ny // 2) * (nz // 2)
    occupied = mask.astype(jnp.float32)[..., None]
    masked = features * mask.astype(jnp.bfloat16)[..., None]
    rimmed = lax.all_gather(with_halo(masked, "space", 1), "head", axis=3, tiled=True)
    whole_masked = lax.slice_in_dim(rimmed, 1, nx + 1, axis=0)
    pre1 = convolve(rimmed, conv1_weight)
    hidden = (occupied * jax.nn.silu(pre1)).astype(jnp.bfloat16)
    pre2 = convolve(with_halo(hidden, "space", 1), conv2_weight)
    refined_all = (occupied * (whole_masked.astype(jnp.float32) + pre2)).astype(jnp.bfloat16)
    refined = lax.dynamic_slice_in_dim(refined_all, member * local, local, 3)
    coarse = jnp.dot(
        to_cells(refined_all),
        down_weight.reshape(8 * chans, width),
        preferred_element_type=jnp.float32,
    ).astype(jnp.bfloat16)
    wide = coarse.astype(jnp.float32)
    normed = (
        wide * lax.rsqrt(jnp.mean(wide * wide, axis=1, keepdims=True) + 1e-05) * norm_gain
    ).astype(jnp.bfloat16)
    local_cols = qkv_weight.shape[2]
    proj = jnp.dot(
        normed, qkv_weight.reshape(width, 3 * local_cols), preferred_element_type=jnp.float32
    )
    proj = proj.astype(jnp.bfloat16).reshape(tokens, 3, local_cols)
    head_size = width // HEADS
    heads_here = local_cols // head_size
    query = proj[:, 0].reshape(tokens, heads_here, head_size)
    live_cell = (
        mask.reshape(nx // 2, 2, ny // 2, 2, nz // 2, 2)
        .max(axis=(1, 3, 5))
        .reshape(1, -1)
        .astype(jnp.bfloat16)
    )
    span = 2 * local_cols
    live_len = -(-tokens // span) * span
    live_rows = jnp.pad(live_cell, ((0, 0), (0, live_len - tokens))).reshape(-1, span)
    live_count = live_rows.shape[0]
    live_rows = jnp.pad(live_rows, ((0, -(-live_count // 8) * 8 - live_count), (0, 0)))
    piece = jnp.concatenate([proj[:, 1], proj[:, 2]], axis=1)
    piece = jnp.concatenate([piece, live_rows], axis=0)
    rows = piece.shape[0]
    gathered = lax.all_gather(piece[None], "space", axis=0, tiled=True)
    parts = gathered.shape[0]
    count = parts * tokens
    piece_keys = gathered[:, :tokens, :local_cols].reshape(count, heads_here, head_size)
    piece_values = gathered[:, :tokens, local_cols:].reshape(count, heads_here, head_size)
    piece_live = (
        gathered[:, tokens : tokens + live_count].reshape(parts, -1)[:, :tokens].reshape(count)
    )
    bias = jnp.where(piece_live > 0, 0.0, -1e30).astype(jnp.float32)
    scale = head_size ** (-0.5)

    def one_block(carry, block):
        top_old, sums, accum = carry
        block_keys, block_values, block_bias = block
        scores = (
            jnp.einsum("qhd,khd->hqk", query, block_keys, preferred_element_type=jnp.float32)
            * scale
            + block_bias[None, None, :]
        )
        top_new = jnp.maximum(top_old, jnp.max(scores, axis=-1))
        expo = jnp.exp(scores - top_new[..., None])
        factor = jnp.exp(top_old - top_new)
        sums = sums * factor + jnp.sum(expo, axis=-1)
        accum = accum * factor[..., None] + jnp.einsum(
            "hqk,khd->hqd",
            expo.astype(jnp.bfloat16),
            block_values,
            preferred_element_type=jnp.float32,
        )
        return ((top_new, sums, accum), None)

    start_state = (
        jnp.full((heads_here, tokens), -1e30, jnp.float32),
        jnp.zeros((heads_here, tokens), jnp.float32),
        jnp.zeros((heads_here, tokens, head_size), jnp.float32),
    )
    size = KEY_BLOCK if count % KEY_BLOCK == 0 else tokens
    blocks = count // size
    stacked = (
        piece_keys.reshape(blocks, size, heads_here, head_size),
        piece_values.reshape(blocks, size, heads_here, head_size),
        bias.reshape(blocks, size),
    )
    carry, unused = lax.scan(one_block, start_state, stacked)
    top_final, sums, accum = carry
    attn = (
        (accum / sums[..., None])
        .transpose(1, 0, 2)
        .reshape(tokens, local_cols)
        .astype(jnp.bfloat16)
    )
    cols_w = lax.all_to_all(out_weight, "head", 1, 0, tiled=True)
    attn_all = lax.all_gather(attn, "head", axis=1, tiled=True)
    mixed = jnp.dot(attn_all, cols_w, preferred_element_type=jnp.float32)
    mine = lax.dynamic_slice_in_dim(wide, member * local_cols, local_cols, 1)
    level_out = (mine + mixed).astype(jnp.bfloat16)
    return (refined, level_out)


def solution(mesh):
    in_specs = (
        P("space", None, None, "head"),
        P("space", None, None),
        P(),
        P(),
        P(),
        P(),
        P(None, None, "head"),
        P("head", None),
    )
    out_specs = (P("space", None, None, "head"), P("space", "head"))
    return jax.shard_map(body, mesh=mesh, in_specs=in_specs, out_specs=out_specs, check_vma=False)
```

profile of v0, /device:TPU:8, one launch (start us, length us, event | category | flops | bytes accessed | tf_op | source)
XLA Modules:
  0.0 343.7 jit_solution(4440227885603397588)
XLA Ops:
  8.2 2.7 copy.59
  11.1 1.7 collective-permute-start
  14.2 3.1 collective-permute-done.1
  17.6 45.3 %all_gather.9 = bf16[10,16,16,128]{2,1,0,3:T(8,128)(2,1)} all-gather(bf16[10,16,16,32]{2,1,0,3:T(8,128)(2,1)S(1)} %pad_maximum_fusion), channel_id=1, replica_groups=mesh['space'=64,'head'=4] {'head'}, dimensions={3}, use_global_device_ids=true | all-gather | bytes 819200 | tf_op jit(solution)/shard_map/all_gather | solution.py:55
  62.9 5.2 %copy.60 = bf16[10,16,16,128]{3,1,2,0:T(8,128)(2,1)S(1)} copy(bf16[10,16,16,128]{2,1,0,3:T(8,128)(2,1)} %all_gather.9) | data formatting | bytes 1310720 | tf_op jit(solution)/shard_map/all_gather | solution.py:55
  69.3 6.2 %fusion.35 = f32[8,16,8,3,128]{4,2,3,1,0:T(8,128)S(1)} fusion(bf16[3,3,3,128,128]{4,3,2,1,0:T(8,128)(2,1)S(1)} %bitcast.110, bf16[10,16,1,7,2,128]{5,3,4,1,0,2:T(8,128)(2,1)S(1)} %slice.51, bf16[10,16,1,8,3,128]{5,3,4,1,0,2:T(8,128)(2,1)S(1)} %copy.63, pred[8,3]{0,1:T(4,128)(4,1)S(1)} %copy-done.7), kind=kOutput, calls=%fused_computation.40 | convolution fusion | flops 2609971200 | bytes 4014104 | tf_op jit(solution)/shard_map/conv_general_dilated | solution.py:28
  76.1 4.3 %collective-permute-start.2 = (bf16[1,16,16,128]{3,1,2,0:T(8,128)(2,1)S(1)}, bf16[1,16,16,128]{3,1,2,0:T(8,128)(2,1)S(1)}, u32[]{:S(2)}, u32[]{:S(2)}) collective-permute-start(bf16[1,16,16,128]{3,1,2,0:T(8,128)(2,1)S(1)} %get-tuple-element.128), channel_id=1, source_target_pairs={{0,4},{4,8},{8,12},{12,16},{16,20},{20,24},{24,28},{28,32},{32,36}... | collective-permute-start | bytes 196616 | tf_op jit(solution)/shard_map/ppermute | solution.py:17
  84.1 1.9 collective-permute-done.3
  87.2 6.2 %fusion.32 = f32[8,16,8,3,128]{4,2,3,1,0:T(8,128)S(1)} fusion(bf16[3,3,3,128,128]{4,3,2,1,0:T(8,128)(2,1)S(1)} %bitcast.111, bf16[10,16,1,7,2,128]{5,3,4,1,0,2:T(8,128)(2,1)S(1)} %slice.55, bf16[10,16,1,8,3,128]{5,3,4,1,0,2:T(8,128)(2,1)S(1)} %copy.66, pred[8,3]{0,1:T(4,128)(4,1)S(1)} %copy-done.7), kind=kOutput, calls=%fused_computation.39 | convolution fusion | flops 2609971200 | bytes 4014104 | tf_op jit(solution)/shard_map/conv_general_dilated | solution.py:28
  97.1 4.5 %all-to-all-start = ((bf16[128,4,128]{0,2,1:T(8,128)(2,1)}), bf16[128,4,128]{0,2,1:T(8,128)(2,1)S(1)}, u32[]{:S(2)}, u32[]{:S(2)}) async-start(bf16[128,4,128]{0,2,1:T(8,128)(2,1)} %bitcast.24), calls=%async_computation | async-start | bytes 262144 | tf_op jit(solution)/shard_map/all_to_all | solution.py:144
  102.7 3.4 all-to-all-done
  106.2 82.1 %all-gather.3.cloned.1.call-done = bf16[16896,256]{1,0:T(8,128)(2,1)} async-done(((bf16[264,256]{1,0:T(8,128)(2,1)}), bf16[16896,256]{1,0:T(8,128)(2,1)}) %all-gather.3.cloned.1.call-update) | async-done | bytes 8650768 | tf_op jit(solution)/shard_map/all_gather | solution.py:93
  189.5 6.0 %fusion.56 = (bf16[64,256,128]{2,1,0:T(8,128)(2,1)}, bf16[64,256,128]{2,1,0:T(8,128)(2,1)}) fusion(bf16[64,264,256]{2,1,0:T(8,128)(2,1)} %bitcast.93), kind=kLoop, calls=%fused_computation.77 | loop fusion | bytes 16777216 | tf_op jit(solution)/shard_map/slice | solution.py:97
  195.5 14.7 %reshape.108 = bf16[16,1024,2,64]{3,2,1,0:T(2,128)(2,1)} reshape(bf16[64,256,128]{2,1,0:T(8,128)(2,1)} %get-tuple-element.124) | data formatting | bytes 8388608 | tf_op jit(solution)/shard_map/reshape;reshape | solution.py:133
  210.2 20.1 %copy.78 = bf16[16,1024,2,64]{1,3,2,0:T(8,128)(2,1)} copy(bf16[16,1024,2,64]{3,2,1,0:T(2,128)(2,1)} %reshape.108) | data formatting | bytes 8388608
  230.3 14.7 %reshape.107 = bf16[16,1024,2,64]{3,2,1,0:T(2,128)(2,1)} reshape(bf16[64,256,128]{2,1,0:T(8,128)(2,1)} %get-tuple-element.125) | data formatting | bytes 8388608 | tf_op jit(solution)/shard_map/reshape;reshape | solution.py:132
  245.0 20.1 %copy.77 = bf16[16,1024,2,64]{1,3,2,0:T(8,128)(2,1)} copy(bf16[16,1024,2,64]{3,2,1,0:T(2,128)(2,1)} %reshape.107) | data formatting | bytes 8388608
  265.1 58.0 %while.15 = (s32[]{:T(128)}, f32[2,256]{1,0:T(2,128)S(1)}, f32[2,256]{1,0:T(2,128)S(1)}, f32[2,256,64]{1,2,0:T(8,128)S(1)}, bf16[16,1024,2,64]{1,3,2,0:T(8,128)(...) while((s32[]{:T(128)}, f32[2,256]{1,0:T(2,128)S(1)}, ...), condition=%wide.region_5.6_spmd.clone, body=%wide.region_2.5_spmd.clone.sunk | while | flops 140085760 | bytes 7196805 | solution.py:136
  270.7 1.6 convolution_add_fusion.3
  274.4 1.6 convolution_add_fusion.3
  278.0 1.6 convolution_add_fusion.3
  285.3 1.6 convolution_add_fusion.3
  288.9 1.6 convolution_add_fusion.3
  323.2 12.8 %all_gather.11 = bf16[256,512]{0,1:T(8,128)(2,1)S(1)} all-gather(bf16[256,128]{0,1:T(8,128)(2,1)S(1)} %bitcast.109), channel_id=1, replica_groups=mesh['space'=64,'head'=4] {'head'}, dimensions={1}, use_global_device_ids=true | all-gather | bytes 327680 | tf_op jit(solution)/shard_map/all_gather | solution.py:145
  (170 shorter events, 65.6 us)
Async XLA Ops:
  7.2 87.3 %copy-start = (bf16[8,128,512]{2,1,0:T(8,128)(2,1)S(1)}, bf16[8,128,512]{2,1,0:T(8,128)(2,1)}, u32[]{:S(2)}) copy-start(bf16[8,128,512]{2,1,0:T(8,128)(2,1)} %param.14) | copy-start | bytes 3145732
  7.2 181.2 %all-gather.3.cloned.1.call-start = ((), (), s32[]{:S(2)}) async-start(), calls=%async_computation.1 | async-start | bytes 8785920 | tf_op jit(solution)/shard_map/all_gather | solution.py:93
  11.1 3.1 collective-permute-start
  12.8 4.5 %collective-permute-start.1 = (bf16[1,16,16,32]{2,1,0,3:T(8,128)(2,1)S(1)}, bf16[1,16,16,32]{2,1,0,3:T(8,128)(2,1)S(1)}, u32[]{:S(2)}, u32[]{:S(2)}) collective-permute-start(bf16[1,16,16,32]{2,1,0,3:T(8,128)(2,1)S(1)} %get-tuple-element.127), channel_id=1, source_target_pairs={{4,0},{8,4},{12,8},{16,12},{20,16},{24,20},{28,24},{32,28},{36,32}... | collective-permute-start | bytes 49160 | tf_op jit(solution)/shard_map/ppermute | solution.py:19
  68.1 1.2 copy-start.5
  68.1 1.2 copy-start.7
  75.5 6.5 %copy-start.2 = (s32[8,16,16]{2,1,0:T(8,128)S(1)}, s32[8,16,16]{2,1,0:T(8,128)}, u32[]{:S(2)}) copy-start(s32[8,16,16]{2,1,0:T(8,128)} %param.11) | copy-start | bytes 24580
  76.1 7.9 %collective-permute-start.2 = (bf16[1,16,16,128]{3,1,2,0:T(8,128)(2,1)S(1)}, bf16[1,16,16,128]{3,1,2,0:T(8,128)(2,1)S(1)}, u32[]{:S(2)}, u32[]{:S(2)}) collective-permute-start(bf16[1,16,16,128]{3,1,2,0:T(8,128)(2,1)S(1)} %get-tuple-element.128), channel_id=1, source_target_pairs={{0,4},{4,8},{8,12},{12,16},{16,20},{20,24},{24,28},{28,32},{32,36}... | collective-permute-start | bytes 196616 | tf_op jit(solution)/shard_map/ppermute | solution.py:17
  80.5 5.5 %collective-permute-start.3 = (bf16[1,16,16,128]{3,1,2,0:T(8,128)(2,1)S(1)}, bf16[1,16,16,128]{3,1,2,0:T(8,128)(2,1)S(1)}, u32[]{:S(2)}, u32[]{:S(2)}) collective-permute-start(bf16[1,16,16,128]{3,1,2,0:T(8,128)(2,1)S(1)} %get-tuple-element.129), channel_id=1, source_target_pairs={{4,0},{8,4},{12,8},{16,12},{20,16},{24,20},{28,24},{32,28},{36,32}... | collective-permute-start | bytes 196616 | tf_op jit(solution)/shard_map/ppermute | solution.py:19
  86.0 1.2 copy-start.6
  94.1 0.9 copy-start.4
  94.4 1.9 copy-start.3
  97.1 9.0 %all-to-all-start = ((bf16[128,4,128]{0,2,1:T(8,128)(2,1)}), bf16[128,4,128]{0,2,1:T(8,128)(2,1)S(1)}, u32[]{:S(2)}, u32[]{:S(2)}) async-start(bf16[128,4,128]{0,2,1:T(8,128)(2,1)} %bitcast.24), calls=%async_computation | async-start | bytes 262144 | tf_op jit(solution)/shard_map/all_to_all | solution.py:144
  323.1 13.7 %copy-start.1 = (bf16[8,128,512]{2,1,0:T(8,128)(2,1)S(1)}, bf16[8,128,512]{2,1,0:T(8,128)(2,1)}, u32[]{:S(2)}) copy-start(bf16[8,128,512]{2,1,0:T(8,128)(2,1)} %param.14) | copy-start | bytes 3145732
Sparse Core Ops, SparseCore 0:
  96.4 91.8 all-gather.2
where the time goes:
time: 347 us; the launch traced here: 344 us
  local copies, waits for them, and re-layouts  91.5 us (26%)
  waiting for transfers between devices  90.5 us (26%)
  matrix products  62.8 us (18%)
  blocking collectives  58.1 us (17%)
  between operations  14.4 us (4%)
  starting transfers between devices  13.4 us (4%)
  other arithmetic  12.2 us (4%)
    all_gather x1, waiting for transfers between devices, body(): gathered = lax.all_gather(piece[None], 'space', axis=0, tiled=True)  82.1 us
    unnamed x22, local copies, waits for them, and re-layouts  46.9 us
    all_gather x1, blocking collectives, body(): lax.all_gather(with_halo(masked, 'space', 1), 'head', axis=3, tiled=True)  45.3 us
    dot_general x16, matrix products, one_block(): jnp.einsum('hqk,khd->hqd', expo.astype(jnp.bfloat16), block_values, prefe...  25.1 us
    dot_general x16, matrix products, one_block(): jnp.einsum('qhd,khd->hqk', query, block_keys, preferred_element_type=jnp....  23.6 us
    another operation x1, local copies, waits for them, and re-layouts, body(): piece_values.reshape(blocks, size, heads_here, head_size)  14.7 us
    another operation x1, local copies, waits for them, and re-layouts, body(): piece_keys.reshape(blocks, size, heads_here, head_size)  14.7 us
    all_gather x1, blocking collectives, body(): attn_all = lax.all_gather(attn, 'head', axis=1, tiled=True)  12.8 us
  transfers between devices with their start and end apart: 6, of which 4 were waited for; matrix products, arithmetic and copies ran while one was open for 1% of the time, Pallas kernels for 0%

commit v1 on v0

--- a/solution.py
+++ b/solution.py
@@ -45,6 +45,18 @@
 def body(
     features, mask, conv1_weight, conv2_weight, down_weight, norm_gain, qkv_weight, out_weight
 ):
+
+    def treat_flows_all(point, axis_id):
+        return jnp.concatenate(
+            jax.lax.all_to_all(
+                jnp.stack(jnp.split(point, jax.lax.axis_size(axis_id), axis=1), axis=0),
+                split_axis=0,
+                concat_axis=0,
+                axis_name=axis_id,
+            ),
+            axis=0,
+        )
+
     member = lax.axis_index("head")
     nx, ny, nz, local = features.shape
     width = down_weight.shape[2]
@@ -141,7 +153,7 @@
         .reshape(tokens, local_cols)
         .astype(jnp.bfloat16)
     )
-    cols_w = lax.all_to_all(out_weight, "head", 1, 0, tiled=True)
+    cols_w = treat_flows_all(out_weight, axis_id="head")
     attn_all = lax.all_gather(attn, "head", axis=1, tiled=True)
     mixed = jnp.dot(attn_all, cols_w, preferred_element_type=jnp.float32)
     mine = lax.dynamic_slice_in_dim(wide, member * local_cols, local_cols, 1)

time: 347 us -> 347 us (level)
    all_gather x1, waiting for transfers between devices: 82.1 us -> 85.7 us  [body(): gathered = lax.all_gather(piece[None], 'space', axis=0, tiled=True)]
    unnamed x22 -> x21, local copies, waits for them, and re-layouts: 46.9 us -> 46.2 us
  transfers between devices with their start and end apart: 6 -> 6, of which waited for: 4 -> 3; matrix products, arithmetic and copies ran while one was open for 1% -> 40% of each run, Pallas kernels for 0% -> 0%
where the time goes in v1:
time: 347 us; the launch traced here: 344 us
  local copies, waits for them, and re-layouts  90.8 us (26%)
  waiting for transfers between devices  90.7 us (26%)
  matrix products  62.8 us (18%)
  blocking collectives  58.1 us (17%)
  between operations  14.4 us (4%)
  starting transfers between devices  13.4 us (4%)
  other arithmetic  12.8 us (4%)
    all_gather x1, waiting for transfers between devices, body(): gathered = lax.all_gather(piece[None], 'space', axis=0, tiled=True)  85.7 us
    unnamed x21, local copies, waits for them, and re-layouts  46.2 us
    all_gather x1, blocking collectives, body(): lax.all_gather(with_halo(masked, 'space', 1), 'head', axis=3, tiled=True)  45.3 us
    dot_general x16, matrix products, one_block(): jnp.einsum('hqk,khd->hqd', expo.astype(jnp.bfloat16), block_values, prefe...  25.1 us
    dot_general x16, matrix products, one_block(): jnp.einsum('qhd,khd->hqk', query, block_keys, preferred_element_type=jnp....  23.6 us
    another operation x1, local copies, waits for them, and re-layouts, body(): piece_values.reshape(blocks, size, heads_here, head_size)  14.7 us
    another operation x1, local copies, waits for them, and re-layouts, body(): piece_keys.reshape(blocks, size, heads_here, head_size)  14.7 us
    all_gather x1, blocking collectives, body(): attn_all = lax.all_gather(attn, 'head', axis=1, tiled=True)  12.8 us
  transfers between devices with their start and end apart: 6, of which 3 were waited for; matrix products, arithmetic and copies ran while one was open for 40% of the time, Pallas kernels for 0%

profile of v1, /device:TPU:8, one launch (start us, length us, event | category | flops | bytes accessed | tf_op | source)
XLA Modules:
  0.0 343.9 jit_solution(16079363204630740678)
XLA Ops:
  8.2 2.7 copy.57
  11.1 1.7 collective-permute-start
  14.2 3.1 collective-permute-done.1
  17.6 45.3 %all_gather.9 = bf16[10,16,16,128]{2,1,0,3:T(8,128)(2,1)} all-gather(bf16[10,16,16,32]{2,1,0,3:T(8,128)(2,1)S(1)} %pad_maximum_fusion), channel_id=1, replica_groups=mesh['space'=64,'head'=4] {'head'}, dimensions={3}, use_global_device_ids=true | all-gather | bytes 819200 | tf_op jit(solution)/shard_map/all_gather | solution.py:67
  62.9 5.2 %copy.58 = bf16[10,16,16,128]{3,1,2,0:T(8,128)(2,1)S(1)} copy(bf16[10,16,16,128]{2,1,0,3:T(8,128)(2,1)} %all_gather.9) | data formatting | bytes 1310720 | tf_op jit(solution)/shard_map/all_gather | solution.py:67
  69.3 6.2 %fusion.35 = f32[8,16,8,3,128]{4,2,3,1,0:T(8,128)S(1)} fusion(bf16[3,3,3,128,128]{4,3,2,1,0:T(8,128)(2,1)S(1)} %bitcast.115, bf16[10,16,1,7,2,128]{5,3,4,1,0,2:T(8,128)(2,1)S(1)} %slice.51, bf16[10,16,1,8,3,128]{5,3,4,1,0,2:T(8,128)(2,1)S(1)} %copy.61, pred[8,3]{0,1:T(4,128)(4,1)S(1)} %copy-done.7), kind=kOutput, calls=%fused_computation.40 | convolution fusion | flops 2609971200 | bytes 4014104 | tf_op jit(solution)/shard_map/conv_general_dilated | solution.py:28
  76.1 4.3 %collective-permute-start.2 = (bf16[1,16,16,128]{3,1,2,0:T(8,128)(2,1)S(1)}, bf16[1,16,16,128]{3,1,2,0:T(8,128)(2,1)S(1)}, u32[]{:S(2)}, u32[]{:S(2)}) collective-permute-start(bf16[1,16,16,128]{3,1,2,0:T(8,128)(2,1)S(1)} %get-tuple-element.128), channel_id=1, source_target_pairs={{0,4},{4,8},{8,12},{12,16},{16,20},{20,24},{24,28},{28,32},{32,36}... | collective-permute-start | bytes 196616 | tf_op jit(solution)/shard_map/ppermute | solution.py:17
  84.1 1.9 collective-permute-done.3
  87.2 6.2 %fusion.32 = f32[8,16,8,3,128]{4,2,3,1,0:T(8,128)S(1)} fusion(bf16[3,3,3,128,128]{4,3,2,1,0:T(8,128)(2,1)S(1)} %bitcast.116, bf16[10,16,1,7,2,128]{5,3,4,1,0,2:T(8,128)(2,1)S(1)} %slice.55, bf16[10,16,1,8,3,128]{5,3,4,1,0,2:T(8,128)(2,1)S(1)} %copy.64, pred[8,3]{0,1:T(4,128)(4,1)S(1)} %copy-done.7), kind=kOutput, calls=%fused_computation.39 | convolution fusion | flops 2609971200 | bytes 4014104 | tf_op jit(solution)/shard_map/conv_general_dilated | solution.py:28
  97.0 4.5 %all-to-all-start = ((bf16[4,128,128]{2,1,0:T(8,128)(2,1)}), bf16[4,128,128]{2,1,0:T(8,128)(2,1)S(1)}, u32[]{:S(2)}, u32[]{:S(2)}) async-start(bf16[4,128,128]{2,1,0:T(8,128)(2,1)} %pad_maximum_fusion.1), calls=%async_computation | async-start | bytes 262144 | tf_op jit(solution)/shard_map/all_to_all | solution.py:51
  102.7 85.7 %all-gather.3.cloned.1.call-done = bf16[16896,256]{1,0:T(8,128)(2,1)} async-done(((bf16[264,256]{1,0:T(8,128)(2,1)}), bf16[16896,256]{1,0:T(8,128)(2,1)}) %all-gather.3.cloned.1.call-update) | async-done | bytes 8650768 | tf_op jit(solution)/shard_map/all_gather | solution.py:105
  189.5 6.0 %fusion.56 = (bf16[64,256,128]{2,1,0:T(8,128)(2,1)}, bf16[64,256,128]{2,1,0:T(8,128)(2,1)}) fusion(bf16[64,264,256]{2,1,0:T(8,128)(2,1)} %bitcast.99), kind=kLoop, calls=%fused_computation.82 | loop fusion | bytes 16777216 | tf_op jit(solution)/shard_map/slice | solution.py:109
  195.5 14.7 %reshape.109 = bf16[16,1024,2,64]{3,2,1,0:T(2,128)(2,1)} reshape(bf16[64,256,128]{2,1,0:T(8,128)(2,1)} %get-tuple-element.124) | data formatting | bytes 8388608 | tf_op jit(solution)/shard_map/reshape;reshape | solution.py:145
  210.2 20.1 %copy.76 = bf16[16,1024,2,64]{1,3,2,0:T(8,128)(2,1)} copy(bf16[16,1024,2,64]{3,2,1,0:T(2,128)(2,1)} %reshape.109) | data formatting | bytes 8388608
  230.3 14.7 %reshape.108 = bf16[16,1024,2,64]{3,2,1,0:T(2,128)(2,1)} reshape(bf16[64,256,128]{2,1,0:T(8,128)(2,1)} %get-tuple-element.125) | data formatting | bytes 8388608 | tf_op jit(solution)/shard_map/reshape;reshape | solution.py:144
  245.0 20.2 %copy.75 = bf16[16,1024,2,64]{1,3,2,0:T(8,128)(2,1)} copy(bf16[16,1024,2,64]{3,2,1,0:T(2,128)(2,1)} %reshape.108) | data formatting | bytes 8388608
  265.2 58.0 %while.15 = (s32[]{:T(128)}, f32[2,256]{1,0:T(2,128)S(1)}, f32[2,256]{1,0:T(2,128)S(1)}, f32[2,256,64]{1,2,0:T(8,128)S(1)}, bf16[16,1024,2,64]{1,3,2,0:T(8,128)(...) while((s32[]{:T(128)}, f32[2,256]{1,0:T(2,128)S(1)}, ...), condition=%wide.region_5.6_spmd.clone, body=%wide.region_2.5_spmd.clone.sunk | while | flops 140085760 | bytes 7196805 | solution.py:148
  274.5 1.6 convolution_add_fusion.3
  281.7 1.6 convolution_add_fusion.3
  285.4 1.6 convolution_add_fusion.3
  292.6 1.6 convolution_add_fusion.3
  296.3 1.6 convolution_add_fusion.3
  299.9 1.6 convolution_add_fusion.3
  323.3 12.8 %all_gather.11 = bf16[256,512]{0,1:T(8,128)(2,1)S(1)} all-gather(bf16[256,128]{0,1:T(8,128)(2,1)S(1)} %bitcast.114), channel_id=1, replica_groups=mesh['space'=64,'head'=4] {'head'}, dimensions={1}, use_global_device_ids=true | all-gather | bytes 327680 | tf_op jit(solution)/shard_map/all_gather | solution.py:157
  (170 shorter events, 63.8 us)
Async XLA Ops:
  7.2 87.3 %copy-start = (bf16[8,128,512]{2,1,0:T(8,128)(2,1)S(1)}, bf16[8,128,512]{2,1,0:T(8,128)(2,1)}, u32[]{:S(2)}) copy-start(bf16[8,128,512]{2,1,0:T(8,128)(2,1)} %param.14) | copy-start | bytes 3145732
  7.2 181.2 %all-gather.3.cloned.1.call-start = ((), (), s32[]{:S(2)}) async-start(), calls=%async_computation.1 | async-start | bytes 8785920 | tf_op jit(solution)/shard_map/all_gather | solution.py:105
  11.1 3.1 collective-permute-start
  12.8 4.5 %collective-permute-start.1 = (bf16[1,16,16,32]{2,1,0,3:T(8,128)(2,1)S(1)}, bf16[1,16,16,32]{2,1,0,3:T(8,128)(2,1)S(1)}, u32[]{:S(2)}, u32[]{:S(2)}) collective-permute-start(bf16[1,16,16,32]{2,1,0,3:T(8,128)(2,1)S(1)} %get-tuple-element.127), channel_id=1, source_target_pairs={{4,0},{8,4},{12,8},{16,12},{20,16},{24,20},{28,24},{32,28},{36,32}... | collective-permute-start | bytes 49160 | tf_op jit(solution)/shard_map/ppermute | solution.py:19
  68.1 1.2 copy-start.5
  68.1 1.2 copy-start.7
  75.5 6.5 %copy-start.2 = (s32[8,16,16]{2,1,0:T(8,128)S(1)}, s32[8,16,16]{2,1,0:T(8,128)}, u32[]{:S(2)}) copy-start(s32[8,16,16]{2,1,0:T(8,128)} %param.11) | copy-start | bytes 24580
  76.1 7.9 %collective-permute-start.2 = (bf16[1,16,16,128]{3,1,2,0:T(8,128)(2,1)S(1)}, bf16[1,16,16,128]{3,1,2,0:T(8,128)(2,1)S(1)}, u32[]{:S(2)}, u32[]{:S(2)}) collective-permute-start(bf16[1,16,16,128]{3,1,2,0:T(8,128)(2,1)S(1)} %get-tuple-element.128), channel_id=1, source_target_pairs={{0,4},{4,8},{8,12},{12,16},{16,20},{20,24},{24,28},{28,32},{32,36}... | collective-permute-start | bytes 196616 | tf_op jit(solution)/shard_map/ppermute | solution.py:17
  80.5 5.5 %collective-permute-start.3 = (bf16[1,16,16,128]{3,1,2,0:T(8,128)(2,1)S(1)}, bf16[1,16,16,128]{3,1,2,0:T(8,128)(2,1)S(1)}, u32[]{:S(2)}, u32[]{:S(2)}) collective-permute-start(bf16[1,16,16,128]{3,1,2,0:T(8,128)(2,1)S(1)} %get-tuple-element.129), channel_id=1, source_target_pairs={{4,0},{8,4},{12,8},{16,12},{20,16},{24,20},{28,24},{32,28},{36,32}... | collective-permute-start | bytes 196616 | tf_op jit(solution)/shard_map/ppermute | solution.py:19
  86.0 1.2 copy-start.6
  94.1 0.9 copy-start.4
  94.4 1.9 copy-start.3
  97.0 239.1 %all-to-all-start = ((bf16[4,128,128]{2,1,0:T(8,128)(2,1)}), bf16[4,128,128]{2,1,0:T(8,128)(2,1)S(1)}, u32[]{:S(2)}, u32[]{:S(2)}) async-start(bf16[4,128,128]{2,1,0:T(8,128)(2,1)} %pad_maximum_fusion.1), calls=%async_computation | async-start | bytes 262144 | tf_op jit(solution)/shard_map/all_to_all | solution.py:51
  323.3 13.8 %copy-start.1 = (bf16[8,128,512]{2,1,0:T(8,128)(2,1)S(1)}, bf16[8,128,512]{2,1,0:T(8,128)(2,1)}, u32[]{:S(2)}) copy-start(bf16[8,128,512]{2,1,0:T(8,128)(2,1)} %param.14) | copy-start | bytes 3145732
Sparse Core Ops, SparseCore 0:
  96.5 91.8 all-gather.2
